TPU v7x, 256 devices: a whole 4x4x8 slice. The times are simulated.
256 devices in a mesh: dp: 8 (over x, core), seq: 32 (over y, z).
Axes of the slice: x: 4, y: 4, z: 8, core: 2. Of those that a mesh axis runs over, the one named last changes fastest.
Arguments:
- activations: bfloat16 [8, 4096, 2048], P('dp', 'seq'), may hold values from -16 to 16
- w_query: bfloat16 [2048, 2048], P('seq')
- w_key: bfloat16 [2048, 256], P('seq')
- w_value: bfloat16 [2048, 256], P('seq'), may hold values from -0.125 to 0.125
- key_blocks: int32 [32, 32, 7], replicated, may hold values from 0 to 31, as said below
- random_count: int32 [32], replicated, may hold values from 1 to 3, 64 in all
- grad_out: bfloat16 [8, 4096, 2048], P('dp', 'seq'), may hold values from -6 to 6
Outputs:
- attn_out: bfloat16 [8, 4096, 2048], P('dp', 'seq')
- grad_x: bfloat16 [8, 4096, 2048], P('dp', 'seq')
- grad_wq: bfloat16 [2048, 2048], P('seq')
- grad_wk: bfloat16 [2048, 256], P('seq')
- grad_wv: bfloat16 [2048, 256], P('seq')
Inputs may be any that keep to these rules, and one draw needn't show every extreme that they name: `key_blocks`: row b of head h: columns 0 to 2 are b - 1, b and b + 1 modulo 32; column 3 is one block of the head, the same in all its rows; columns 4 to 6 are three blocks that differ from each other and from the row's first four entries. Head h uses the first random_count[h] of its three random key blocks; the counts sum to 64.
All inputs are finite; a program needn't handle non-finite values.
Results may differ from a plain program's by a relative error of at most 0.025.
The roundings to bfloat16 on the way count: a program that leaves them out, or rounds other values in their place, can miss the bound.
Values may be sent and summed in bfloat16 or wider, within the bound.
No kernel may reach another device: no remote copies, remote signals or barrier semaphores. Data moves between devices by JAX's collectives and lax.ppermute only.
A program may use at most 128 MiB of HBM per device.

v0:
```python
import math
import jax
import jax.numpy as jnp
from jax import lax
from jax.sharding import PartitionSpec as P

HD = 64
GROUP = 8
masked_score = -1e30
query_group = 4
RING_Z = 8


def head_pass(queries, key_rows, value_rows, grad_head, blocks, extra_count):
    seq_len, head_width = queries.shape
    block_count, slot_count = blocks.shape
    block_len = seq_len // block_count
    score_scale = head_width ** (-0.5)
    key_tiles = key_rows.reshape(block_count, block_len, head_width)
    value_tiles = value_rows.reshape(block_count, block_len, head_width)
    q_part = queries.reshape(block_count, block_len, head_width)
    g_part = grad_head.reshape(block_count, block_len, head_width)
    usable = jnp.repeat(jnp.arange(slot_count) < 4 + extra_count, block_len)
    k_part = key_tiles[blocks].reshape(block_count, slot_count * block_len, head_width)
    v_part = value_tiles[blocks].reshape(block_count, slot_count * block_len, head_width)
    scores = (
        jnp.einsum("gqe,gke->gqk", q_part, k_part, preferred_element_type=jnp.float32) * score_scale
    )
    scores = jnp.where(usable, scores, masked_score)
    highest = jnp.max(scores, axis=-1, keepdims=True)
    exponent = jnp.exp(scores - highest)
    shares = exponent / jnp.sum(exponent, axis=-1, keepdims=True)
    shares_low = shares.astype(jnp.bfloat16)
    attended = jnp.einsum(
        "gqk,gke->gqe", shares_low, v_part, preferred_element_type=jnp.float32
    ).astype(jnp.bfloat16)
    grad_shares = jnp.einsum("gqe,gke->gqk", g_part, v_part, preferred_element_type=jnp.float32)
    weighted = jnp.sum(grad_shares * shares, axis=-1, keepdims=True)
    grad_scores = (shares * (grad_shares - weighted)).astype(jnp.bfloat16)
    grad_query = (
        jnp.einsum("gqk,gke->gqe", grad_scores, k_part, preferred_element_type=jnp.float32)
        * score_scale
    ).astype(jnp.bfloat16)
    grad_keys = (
        jnp.einsum("gqk,gqe->gke", grad_scores, q_part, preferred_element_type=jnp.float32)
        * score_scale
    )
    grad_values = jnp.einsum("gqk,gqe->gke", shares_low, g_part, preferred_element_type=jnp.float32)
    pieces = jnp.concatenate([grad_keys, grad_values], axis=-1).reshape(
        block_count * slot_count, block_len * 2 * head_width
    )
    owner = (
        blocks.reshape(1, block_count * slot_count)
        == jnp.arange(block_count, dtype=blocks.dtype)[:, None]
    ).astype(jnp.float32)
    summed = jnp.dot(owner, pieces, precision=lax.Precision.HIGHEST)
    return (
        attended.reshape(seq_len, head_width),
        grad_query.reshape(seq_len, head_width),
        summed.reshape(seq_len, 2 * head_width),
    )


def ring_reduce_scatter(parts, ring, stride, position):
    seq_devices = lax.axis_size("seq")
    group = ring * stride
    me = position // stride % ring
    width = parts.shape[-1] // 2
    ahead = [
        (s, s // group * group + (s // stride % ring + 1) % ring * stride + s % stride)
        for s in range(seq_devices)
    ]
    behind = [(b, a) for a, b in ahead]
    total = []
    for side, perm, sign in ((0, ahead, 1), (1, behind, -1)):
        own = parts[..., side * width : (side + 1) * width]

        def chunk(k):
            return lax.dynamic_index_in_dim(own, (me - sign * (1 + k)) % ring, 0, keepdims=False)

        buf = chunk(0)
        for k in range(ring - 1):
            got = lax.ppermute(buf, "seq", perm)
            buf = (got.astype(jnp.float32) + chunk(k + 1).astype(jnp.float32)).astype(jnp.bfloat16)
        total.append(buf)
    return jnp.concatenate(total, axis=-1)


def per_device(activations, w_query, w_key, w_value, key_blocks, random_count, grad_out):
    seq_devices = lax.axis_size("seq")
    dp_devices = lax.axis_size("dp")
    position = lax.axis_index("seq")
    dp_index = lax.axis_index("dp")
    tokens = activations[0]
    grad_rows = grad_out[0]
    tok_count = tokens.shape[0]
    heads = w_query.shape[1] // HD
    kv_heads = w_key.shape[1] // HD
    query_cols = heads * HD
    kv_cols = kv_heads * HD
    all_cols = query_cols + 2 * kv_cols
    w_local = jnp.concatenate([w_query, w_key, w_value], axis=1)
    w_full = lax.all_gather(w_local, "seq", axis=0, tiled=True)
    projected = jnp.dot(tokens, w_full, preferred_element_type=jnp.float32).astype(jnp.bfloat16)
    queries = projected[:, :query_cols]
    key_proj = projected[:, query_cols : query_cols + kv_cols]
    value_proj = projected[:, query_cols + kv_cols :]
    query_pieces = queries.reshape(tok_count, heads, HD).transpose(1, 0, 2)
    grad_pieces = grad_rows.reshape(tok_count, heads, HD).transpose(1, 0, 2)
    paired = jnp.concatenate(
        [key_proj.reshape(tok_count, kv_heads, HD), value_proj.reshape(tok_count, kv_heads, HD)],
        axis=2,
    )
    kv_pieces = jnp.repeat(paired.transpose(1, 0, 2), GROUP, axis=0)
    sent = jnp.concatenate([query_pieces, grad_pieces, kv_pieces], axis=2)
    landed = lax.all_to_all(sent, "seq", split_axis=0, concat_axis=1, tiled=True)[0]
    head_q = landed[:, :HD]
    head_grad = landed[:, HD : 2 * HD]
    head_k = landed[:, 2 * HD : 3 * HD]
    head_v = landed[:, 3 * HD :]
    blocks_mine = lax.dynamic_index_in_dim(key_blocks, position, 0, keepdims=False)
    count_mine = lax.dynamic_index_in_dim(random_count, position, 0, keepdims=False)
    attended, grad_query, grad_kv = head_pass(
        head_q, head_k, head_v, head_grad, blocks_mine, count_mine
    )
    back_sent = jnp.concatenate(
        [
            attended.reshape(seq_devices, tok_count, HD),
            grad_query.reshape(seq_devices, tok_count, HD),
            grad_kv.astype(jnp.bfloat16).reshape(seq_devices, tok_count, 2 * HD),
        ],
        axis=2,
    )
    back = lax.all_to_all(back_sent, "seq", split_axis=0, concat_axis=0, tiled=True)
    back_out = back[:, :, :HD]
    back_query = back[:, :, HD : 2 * HD]
    back_kv = back[:, :, 2 * HD :]
    out_rows = back_out.transpose(1, 0, 2).reshape(tok_count, heads * HD)
    grad_q_rows = back_query.transpose(1, 0, 2).reshape(tok_count, heads * HD)
    kv_sum = jnp.sum(
        back_kv.reshape(kv_heads, GROUP, tok_count, 2 * HD), axis=1, dtype=jnp.float32
    ).astype(jnp.bfloat16)
    grad_k_rows = kv_sum[:, :, :HD].transpose(1, 0, 2).reshape(tok_count, kv_heads * HD)
    grad_v_rows = kv_sum[:, :, HD:].transpose(1, 0, 2).reshape(tok_count, kv_heads * HD)
    combined = jnp.concatenate([grad_q_rows, grad_k_rows, grad_v_rows], axis=1)
    contract = (((1,), (1,)), ((), ()))
    grad_x_rows = lax.dot_general(
        combined, w_full, contract, preferred_element_type=jnp.float32
    ).astype(jnp.bfloat16)
    factor = 1.0 / math.sqrt(tok_count * seq_devices * dp_devices)
    over_tokens = (((0,), (0,)), ((), ()))
    term = (
        lax.dot_general(tokens, combined, over_tokens, preferred_element_type=jnp.float32) * factor
    ).astype(jnp.bfloat16)
    half = all_cols // 2
    core = dp_index % 2
    pairs = [(i, i ^ 1) for i in range(dp_devices)]
    keep = lax.dynamic_slice_in_dim(term, core * half, half, axis=1)
    give = lax.dynamic_slice_in_dim(term, (1 - core) * half, half, axis=1)
    got = lax.ppermute(give, "dp", pairs)
    chip_sum = (keep.astype(jnp.float32) + got.astype(jnp.float32)).astype(jnp.bfloat16)
    rows = chip_sum.shape[0] // seq_devices
    by_z = chip_sum.reshape(seq_devices // RING_Z, RING_Z, rows, half).transpose(1, 0, 2, 3)
    by_y = ring_reduce_scatter(by_z, RING_Z, 1, position)
    part = ring_reduce_scatter(by_y, seq_devices // RING_Z, RING_Z, position)
    step = 2
    while step < dp_devices:
        mates = [(i, i ^ step) for i in range(dp_devices)]
        other = lax.ppermute(part, "dp", mates)
        part = (part.astype(jnp.float32) + other.astype(jnp.float32)).astype(jnp.bfloat16)
        step *= 2
    other_half = lax.ppermute(part, "dp", pairs)
    first = jnp.where(core == 0, part, other_half)
    second = jnp.where(core == 0, other_half, part)
    grad_all = jnp.concatenate([first, second], axis=1)
    grad_wq = grad_all[:, :query_cols]
    grad_wk = grad_all[:, query_cols : query_cols + kv_cols]
    grad_wv = grad_all[:, query_cols + kv_cols :]
    return (out_rows[None], grad_x_rows[None], grad_wq, grad_wk, grad_wv)


def solution(mesh):
    placed = (
        P("dp", "seq", None),
        P("seq", None),
        P("seq", None),
        P("seq", None),
        P(),
        P(),
        P("dp", "seq", None),
    )
    return jax.shard_map(
        per_device,
        mesh=mesh,
        in_specs=placed,
        out_specs=(
            P("dp", "seq", None),
            P("dp", "seq", None),
            P("seq", None),
            P("seq", None),
            P("seq", None),
        ),
        check_vma=False,
    )
```

profile of v0, /device:TPU:1, one launch (start us, length us, event | category | flops | bytes accessed | tf_op | source)
XLA Modules:
  0.0 566.1 jit_solution(12210671963242412984)
XLA Ops:
  10.4 113.4 %all-gather.2.cloned.1.call-done = bf16[2048,2560]{1,0:T(8,128)(2,1)} async-done(((bf16[64,2560]{1,0:T(8,128)(2,1)}), bf16[2048,2560]{1,0:T(8,128)(2,1)}) %all-gather.2.cloned.1.call-update) | async-done | bytes 10485776 | tf_op jit(solution)/shard_map/all_gather | solution.py:103
  123.7 6.9 %fusion.13 = bf16[128,2560]{0,1:T(8,128)(2,1)S(1)} fusion(bf16[2048,2560]{1,0:T(8,128)(2,1)} %all-gather.2.cloned.1.call-done, bf16[1,128,2048]{2,1,0:T(8,128)(2,1)S(1)} %copy-done), kind=kOutput, calls=%fused_computation.27 | convolution fusion | flops 1342504960 | bytes 11665408 | tf_op jit(solution)/shard_map/dot_general | solution.py:104
  132.5 5.6 all-to-all-start
  140.7 46.1 %all-to-all-done = bf16[32,128,256]{1,2,0:T(8,128)(2,1)} async-done(((bf16[32,128,256]{1,2,0:T(8,128)(2,1)}), bf16[32,128,256]{1,2,0:T(8,128)(2,1)}, u32[]{:S(2)}, u32[]{:S(2)}) %all-to-all-start) | async-done | bytes 2097184 | tf_op jit(solution)/shard_map/all_to_all | solution.py:116
  198.8 6.2 %copy.122 = bf16[224,128,64]{1,0,2:T(8,128)(2,1)} copy(bf16[224,128,64]{1,2,0:T(8,128)(2,1)} %gather_fusion) | data formatting | bytes 7340032 | tf_op jit(solution)/shard_map/gather | solution.py:24
  205.0 7.8 %reshape.152 = bf16[32,896,64]{1,0,2:T(8,128)(2,1)} reshape(bf16[224,128,64]{1,0,2:T(8,128)(2,1)} %copy.122) | data formatting | bytes 7340032 | tf_op jit(solution)/shard_map/reshape | solution.py:24
  215.8 6.2 %copy.127 = bf16[224,128,64]{1,0,2:T(8,128)(2,1)} copy(bf16[224,128,64]{1,2,0:T(8,128)(2,1)} %gather_fusion.1) | data formatting | bytes 7340032 | tf_op jit(solution)/shard_map/gather | solution.py:25
  222.0 7.8 %reshape.154 = bf16[32,896,64]{1,0,2:T(8,128)(2,1)} reshape(bf16[224,128,64]{1,0,2:T(8,128)(2,1)} %copy.127) | data formatting | bytes 7340032 | tf_op jit(solution)/shard_map/reshape | solution.py:25
  229.8 10.8 %fusion.77 = (f32[32,128]{1,0:T(8,128)S(1)}, f32[32,128,896]{2,1,0:T(8,128)}) fusion(pred[896]{0:T(1024)(128)(4,1)S(1)} %broadcast_bitcast_fusion, bf16[32,128,64]{2,1,0:T(8,128)(2,1)S(1)} %bitcast.152, bf16[32,896,64]{1,0,2:T(8,128)(2,1)} %reshape.152), kind=kOutput, calls=%fused_computation.119 | convolution fusion | flops 484443008 | bytes 18891648 | tf_op jit(solution)/shard_map/sub | solution.py:31
  240.6 9.3 %fusion.31 = bf16[32,128,64]{1,2,0:T(8,128)(2,1)S(1)} fusion(bf16[32,896,64]{1,0,2:T(8,128)(2,1)} %reshape.154, f32[32,128,896]{2,1,0:T(8,128)} %get-tuple-element.49, f32[32,128]{1,0:T(8,128)S(1)} %get-tuple-element.48), kind=kOutput, calls=%fused_computation.42 | convolution fusion | flops 477364224 | bytes 18890752 | tf_op jit(solution)/shard_map/gqk,gke->gqe/dot_general | solution.py:34
  249.9 9.8 %fusion.9 = f32[32,896,64]{1,2,0:T(8,128)} fusion(bf16[32,128,64]{2,1,0:T(8,128)(2,1)S(1)} %bitcast.162, f32[32,128,896]{2,1,0:T(8,128)} %get-tuple-element.49, f32[32,128]{1,0:T(8,128)S(1)} %get-tuple-element.48), kind=kOutput, calls=%fused_computation.22 | convolution fusion | flops 477102080 | bytes 22560768 | tf_op jit(solution)/shard_map/gqk,gqe->gke/dot_general | solution.py:48
  259.7 11.0 %multiply_reduce_fusion = (f32[32,128]{1,0:T(8,128)S(1)}, f32[32,128,896]{2,1,0:T(8,128)}) fusion(f32[32,128,896]{2,1,0:T(8,128)} %get-tuple-element.49, f32[32,128]{1,0:T(8,128)S(1)} %get-tuple-element.48, bf16[32,128,64]{2,1,0:T(8,128)(2,1)S(1)} %bitcast.163, bf16[32,896,64]{1,0,2:T(8,128)(2,1)S(1)} %copy-done.7), kind=kOutput, calls=%fused_computation.9 | convolution fusion | flops 480768000 | bytes 33587200 | tf_op jit(solution)/shard_map/gqe,gke->gqk/dot_general | solution.py:37
  270.7 10.8 %multiply_convert_fusion.1 = bf16[32,128,896]{2,1,0:T(8,128)(2,1)S(1)} fusion(f32[32,128,896]{2,1,0:T(8,128)} %get-tuple-element.51, f32[32,128]{1,0:T(8,128)S(1)} %get-tuple-element.50, f32[32,128,896]{2,1,0:T(8,128)} %get-tuple-element.49, f32[32,128]{1,0:T(8,128)S(1)} %get-tuple-element.48), kind=kLoop, calls=%fused_computation.8 | loop fusion | flops 14680064 | bytes 36732928 | tf_op jit(solution)/shard_map/convert_element_type | solution.py:39
  290.8 10.5 %pad_maximum_fusion = f32[32,896,128]{1,2,0:T(8,128)} fusion(f32[32,896,64]{1,2,0:T(8,128)} %fusion.9, f32[32,896,64]{1,2,0:T(8,128)} %broadcast_multiply_fusion), kind=kLoop, calls=%fused_computation.7 | loop fusion | flops 3670016 | bytes 29360128 | tf_op jit(solution)/shard_map/concatenate | solution.py:49
  301.3 16.1 %copy.136 = f32[32,896,128]{2,1,0:T(8,128)} copy(f32[32,896,128]{1,2,0:T(8,128)} %pad_maximum_fusion) | data formatting | bytes 29360128 | tf_op jit(solution)/shard_map/concatenate | solution.py:49
  317.4 16.0 %reshape.156 = f32[224,16384]{1,0:T(8,128)} reshape(f32[32,896,128]{2,1,0:T(8,128)} %copy.136) | data formatting | bytes 29360128 | tf_op jit(solution)/shard_map/reshape | solution.py:49
  335.1 9.1 %fusion.22 = bf16[32,128,128]{2,0,1:T(8,128)(2,1)S(1)} fusion(s32[224]{0:T(256)S(1)} %eq.47, f32[224,16384]{1,0:T(8,128)} %reshape.156), kind=kOutput, calls=%fused_computation.39 | convolution fusion | flops 1409817600 | bytes 15729536 | tf_op jit(solution)/shard_map/dot_general | solution.py:56
  347.9 7.1 %all-to-all-start.1 = ((bf16[32,128,256]{2,1,0:T(8,128)(2,1)}), bf16[32,128,256]{2,1,0:T(8,128)(2,1)S(1)}, u32[]{:S(2)}, u32[]{:S(2)}) async-start(bf16[32,128,256]{2,1,0:T(8,128)(2,1)} %copy.140), calls=%async_computation.1 | async-start | bytes 4194304 | tf_op jit(solution)/shard_map/all_to_all | solution.py:134
  355.0 48.6 %all-to-all-done.1 = bf16[32,128,256]{2,1,0:T(8,128)(2,1)S(1)} async-done(((bf16[32,128,256]{2,1,0:T(8,128)(2,1)}), bf16[32,128,256]{2,1,0:T(8,128)(2,1)S(1)}, u32[]{:S(2)}, u32[]{:S(2)}) %all-to-all-start.1) | async-done | bytes 2097184 | tf_op jit(solution)/shard_map/all_to_all | solution.py:134
  420.3 8.6 %collective-permute-done = bf16[2048,1280]{1,0:T(8,128)(2,1)} collective-permute-done((bf16[2048,1280]{1,0:T(8,128)(2,1)}, bf16[2048,1280]{1,0:T(8,128)(2,1)}, u32[]{:S(2)}, u32[]{:S(2)}) %collective-permute-start) | collective-permute-done | bytes 5242912 | tf_op jit(solution)/shard_map/ppermute | solution.py:160
  428.9 5.4 fusion.5
  439.9 7.0 %collective-permute-done.11 = bf16[4,64,640]{2,1,0:T(8,128)(2,1)} collective-permute-done((bf16[4,64,640]{2,1,0:T(8,128)(2,1)}, bf16[4,64,640]{2,1,0:T(8,128)(2,1)}, u32[]{:S(2)}, u32[]{:S(2)}) %collective-permute-start.11) | collective-permute-done | bytes 327712 | tf_op jit(solution)/shard_map/ppermute | solution.py:83
  534.7 13.0 %collective-permute-start.23 = (bf16[64,1280]{1,0:T(8,128)(2,1)S(1)}, bf16[64,1280]{1,0:T(8,128)(2,1)S(1)}, u32[]{:S(2)}, u32[]{:S(2)}) collective-permute-start(bf16[64,1280]{1,0:T(8,128)(2,1)S(1)} %add_convert_fusion), channel_id=1, source_target_pairs={{0,32},{32,0},{64,96},{96,64},{128,160},{160,128},{192,224},{224,1... | collective-permute-start | bytes 491528 | tf_op jit(solution)/shard_map/ppermute | solution.py:172
  547.7 8.5 %fusion.21 = bf16[1,128,2048]{2,1,0:T(8,128)(2,1)} fusion(bf16[2048,2560]{1,0:T(8,128)(2,1)} %all-gather.2.cloned.1.call-done, bf16[128,256]{0,1:T(8,128)(2,1)S(1)} %bitcast.165, bf16[128,256]{0,1:T(8,128)(2,1)S(1)} %bitcast.167, bf16[128,2048]{0,1:T(8,128)(2,1)} %bitcast.155), kind=kOutput, calls=%fused_computation.36 | convolution fusion | flops 1344405504 | bytes 11665408 | tf_op jit(solution)/shard_map/dot_general | solution.py:147
  (140 shorter events, 148.9 us)
Async XLA Ops:
  7.2 116.6 %all-gather.2.cloned.1.call-start = ((), (), s32[]{:S(2)}) async-start(), calls=%async_computation.2 | async-start | bytes 10813440 | tf_op jit(solution)/shard_map/all_gather | solution.py:103
  132.5 54.2 %all-to-all-start = ((bf16[32,128,256]{1,2,0:T(8,128)(2,1)}), bf16[32,128,256]{1,2,0:T(8,128)(2,1)}, u32[]{:S(2)}, u32[]{:S(2)}) async-start(bf16[32,128,256]{1,2,0:T(8,128)(2,1)} %pad_maximum_fusion.1), calls=%async_computation | async-start | bytes 4194304 | tf_op jit(solution)/shard_map/all_to_all | solution.py:116
  347.9 55.8 %all-to-all-start.1 = ((bf16[32,128,256]{2,1,0:T(8,128)(2,1)}), bf16[32,128,256]{2,1,0:T(8,128)(2,1)S(1)}, u32[]{:S(2)}, u32[]{:S(2)}) async-start(bf16[32,128,256]{2,1,0:T(8,128)(2,1)} %copy.140), calls=%async_computation.1 | async-start | bytes 4194304 | tf_op jit(solution)/shard_map/all_to_all | solution.py:134
  417.8 11.1 %collective-permute-start = (bf16[2048,1280]{1,0:T(8,128)(2,1)}, bf16[2048,1280]{1,0:T(8,128)(2,1)}, u32[]{:S(2)}, u32[]{:S(2)}) collective-permute-start(bf16[2048,1280]{1,0:T(8,128)(2,1)} %dynamic-slice_bitcast_fusion), channel_id=1, source_target_pairs={{0,32},{32,0},{64,96},{96,64},{128,160},{160,128},{192,224},{224,1... | collective-permute-start | bytes 15728648 | tf_op jit(solution)/shard_map/ppermute | solution.py:160
  437.7 9.2 %collective-permute-start.11 = (bf16[4,64,640]{2,1,0:T(8,128)(2,1)}, bf16[4,64,640]{2,1,0:T(8,128)(2,1)}, u32[]{:S(2)}, u32[]{:S(2)}) collective-permute-start(bf16[4,64,640]{2,1,0:T(8,128)(2,1)} %dynamic-slice_bitcast_fusion.1), channel_id=1, source_target_pairs={{1,0},{2,1},{3,2},{4,3},{5,4},{6,5},{7,6},{0,7},{9,8},{10,9},{11,1... | collective-permute-start | bytes 983048 | tf_op jit(solution)/shard_map/ppermute | solution.py:83
  438.9 11.7 %collective-permute-start.1 = (bf16[4,64,640]{2,1,0:T(8,128)(2,1)}, bf16[4,64,640]{2,1,0:T(8,128)(2,1)}, u32[]{:S(2)}, u32[]{:S(2)}) collective-permute-start(bf16[4,64,640]{2,1,0:T(8,128)(2,1)} %dynamic-slice_bitcast_fusion.2), channel_id=1, source_target_pairs={{0,1},{1,2},{2,3},{3,4},{4,5},{5,6},{6,7},{7,0},{8,9},{9,10},{10,1... | collective-permute-start | bytes 983048 | tf_op jit(solution)/shard_map/ppermute | solution.py:83
  448.8 8.5 %collective-permute-start.12 = (bf16[4,64,640]{2,1,0:T(8,128)(2,1)}, bf16[4,64,640]{2,1,0:T(8,128)(2,1)}, u32[]{:S(2)}, u32[]{:S(2)}) collective-permute-start(bf16[4,64,640]{2,1,0:T(8,128)(2,1)} %fusion.46), channel_id=1, source_target_pairs={{1,0},{2,1},{3,2},{4,3},{5,4},{6,5},{7,6},{0,7},{9,8},{10,9},{11,1... | collective-permute-start | bytes 983048 | tf_op jit(solution)/shard_map/ppermute | solution.py:83
  452.5 9.6 %collective-permute-start.2 = (bf16[4,64,640]{2,1,0:T(8,128)(2,1)}, bf16[4,64,640]{2,1,0:T(8,128)(2,1)}, u32[]{:S(2)}, u32[]{:S(2)}) collective-permute-start(bf16[4,64,640]{2,1,0:T(8,128)(2,1)} %fusion.53), channel_id=1, source_target_pairs={{0,1},{1,2},{2,3},{3,4},{4,5},{5,6},{6,7},{7,0},{8,9},{9,10},{10,1... | collective-permute-start | bytes 983048 | tf_op jit(solution)/shard_map/ppermute | solution.py:83
  459.2 8.1 %collective-permute-start.13 = (bf16[4,64,640]{2,1,0:T(8,128)(2,1)}, bf16[4,64,640]{2,1,0:T(8,128)(2,1)}, u32[]{:S(2)}, u32[]{:S(2)}) collective-permute-start(bf16[4,64,640]{2,1,0:T(8,128)(2,1)} %fusion.45), channel_id=1, source_target_pairs={{1,0},{2,1},{3,2},{4,3},{5,4},{6,5},{7,6},{0,7},{9,8},{10,9},{11,1... | collective-permute-start | bytes 983048 | tf_op jit(solution)/shard_map/ppermute | solution.py:83
  463.9 8.7 %collective-permute-start.3 = (bf16[4,64,640]{2,1,0:T(8,128)(2,1)}, bf16[4,64,640]{2,1,0:T(8,128)(2,1)}, u32[]{:S(2)}, u32[]{:S(2)}) collective-permute-start(bf16[4,64,640]{2,1,0:T(8,128)(2,1)} %fusion.52), channel_id=1, source_target_pairs={{0,1},{1,2},{2,3},{3,4},{4,5},{5,6},{6,7},{7,0},{8,9},{9,10},{10,1... | collective-permute-start | bytes 983048 | tf_op jit(solution)/shard_map/ppermute | solution.py:83
  469.2 7.7 %collective-permute-start.14 = (bf16[4,64,640]{2,1,0:T(8,128)(2,1)}, bf16[4,64,640]{2,1,0:T(8,128)(2,1)}, u32[]{:S(2)}, u32[]{:S(2)}) collective-permute-start(bf16[4,64,640]{2,1,0:T(8,128)(2,1)} %fusion.44), channel_id=1, source_target_pairs={{1,0},{2,1},{3,2},{4,3},{5,4},{6,5},{7,6},{0,7},{9,8},{10,9},{11,1... | collective-permute-start | bytes 983048 | tf_op jit(solution)/shard_map/ppermute | solution.py:83
  474.4 7.5 %collective-permute-start.4 = (bf16[4,64,640]{2,1,0:T(8,128)(2,1)}, bf16[4,64,640]{2,1,0:T(8,128)(2,1)}, u32[]{:S(2)}, u32[]{:S(2)}) collective-permute-start(bf16[4,64,640]{2,1,0:T(8,128)(2,1)} %fusion.51), channel_id=1, source_target_pairs={{0,1},{1,2},{2,3},{3,4},{4,5},{5,6},{6,7},{7,0},{8,9},{9,10},{10,1... | collective-permute-start | bytes 983048 | tf_op jit(solution)/shard_map/ppermute | solution.py:83
  478.8 7.5 %collective-permute-start.15 = (bf16[4,64,640]{2,1,0:T(8,128)(2,1)}, bf16[4,64,640]{2,1,0:T(8,128)(2,1)}, u32[]{:S(2)}, u32[]{:S(2)}) collective-permute-start(bf16[4,64,640]{2,1,0:T(8,128)(2,1)} %fusion.43), channel_id=1, source_target_pairs={{1,0},{2,1},{3,2},{4,3},{5,4},{6,5},{7,6},{0,7},{9,8},{10,9},{11,1... | collective-permute-start | bytes 983048 | tf_op jit(solution)/shard_map/ppermute | solution.py:83
  483.7 7.5 %collective-permute-start.5 = (bf16[4,64,640]{2,1,0:T(8,128)(2,1)}, bf16[4,64,640]{2,1,0:T(8,128)(2,1)}, u32[]{:S(2)}, u32[]{:S(2)}) collective-permute-start(bf16[4,64,640]{2,1,0:T(8,128)(2,1)} %fusion.50), channel_id=1, source_target_pairs={{0,1},{1,2},{2,3},{3,4},{4,5},{5,6},{6,7},{7,0},{8,9},{9,10},{10,1... | collective-permute-start | bytes 983048 | tf_op jit(solution)/shard_map/ppermute | solution.py:83
  488.1 7.5 %collective-permute-start.16 = (bf16[4,64,640]{2,1,0:T(8,128)(2,1)}, bf16[4,64,640]{2,1,0:T(8,128)(2,1)}, u32[]{:S(2)}, u32[]{:S(2)}) collective-permute-start(bf16[4,64,640]{2,1,0:T(8,128)(2,1)} %fusion.42), channel_id=1, source_target_pairs={{1,0},{2,1},{3,2},{4,3},{5,4},{6,5},{7,6},{0,7},{9,8},{10,9},{11,1... | collective-permute-start | bytes 983048 | tf_op jit(solution)/shard_map/ppermute | solution.py:83
  493.0 7.5 %collective-permute-start.6 = (bf16[4,64,640]{2,1,0:T(8,128)(2,1)}, bf16[4,64,640]{2,1,0:T(8,128)(2,1)}, u32[]{:S(2)}, u32[]{:S(2)}) collective-permute-start(bf16[4,64,640]{2,1,0:T(8,128)(2,1)} %fusion.49), channel_id=1, source_target_pairs={{0,1},{1,2},{2,3},{3,4},{4,5},{5,6},{6,7},{7,0},{8,9},{9,10},{10,1... | collective-permute-start | bytes 983048 | tf_op jit(solution)/shard_map/ppermute | solution.py:83
  497.4 7.5 %collective-permute-start.17 = (bf16[4,64,640]{2,1,0:T(8,128)(2,1)}, bf16[4,64,640]{2,1,0:T(8,128)(2,1)}, u32[]{:S(2)}, u32[]{:S(2)}) collective-permute-start(bf16[4,64,640]{2,1,0:T(8,128)(2,1)} %fusion.41), channel_id=1, source_target_pairs={{1,0},{2,1},{3,2},{4,3},{5,4},{6,5},{7,6},{0,7},{9,8},{10,9},{11,1... | collective-permute-start | bytes 983048 | tf_op jit(solution)/shard_map/ppermute | solution.py:83
  501.6 8.4 %collective-permute-start.7 = (bf16[4,64,640]{2,1,0:T(8,128)(2,1)S(1)}, bf16[4,64,640]{2,1,0:T(8,128)(2,1)S(1)}, u32[]{:S(2)}, u32[]{:S(2)}) collective-permute-start(bf16[4,64,640]{2,1,0:T(8,128)(2,1)S(1)} %fusion.48), channel_id=1, source_target_pairs={{0,1},{1,2},{2,3},{3,4},{4,5},{5,6},{6,7},{7,0},{8,9},{9,10},{10,1... | collective-permute-start | bytes 983048 | tf_op jit(solution)/shard_map/ppermute | solution.py:83
  506.1 5.2 collective-permute-start.18
  510.1 4.9 collective-permute-start.8
  515.0 4.6 collective-permute-start.9
  519.6 4.6 collective-permute-start.10
  528.8 5.8 %collective-permute-start.22 = (bf16[64,1280]{1,0:T(8,128)(2,1)S(1)}, bf16[64,1280]{1,0:T(8,128)(2,1)S(1)}, u32[]{:S(2)}, u32[]{:S(2)}) collective-permute-start(bf16[64,1280]{1,0:T(8,128)(2,1)S(1)} %add_convert_fusion.1), channel_id=1, source_target_pairs={{0,128},{32,160},{64,192},{96,224},{128,0},{160,32},{192,64},{224,... | collective-permute-start | bytes 491528 | tf_op jit(solution)/shard_map/ppermute | solution.py:169
  534.7 22.9 %collective-permute-start.23 = (bf16[64,1280]{1,0:T(8,128)(2,1)S(1)}, bf16[64,1280]{1,0:T(8,128)(2,1)S(1)}, u32[]{:S(2)}, u32[]{:S(2)}) collective-permute-start(bf16[64,1280]{1,0:T(8,128)(2,1)S(1)} %add_convert_fusion), channel_id=1, source_target_pairs={{0,32},{32,0},{64,96},{96,64},{128,160},{160,128},{192,224},{224,1... | collective-permute-start | bytes 491528 | tf_op jit(solution)/shard_map/ppermute | solution.py:172
  (14 other events, 224.5 us)
Sparse Core Ops, SparseCore 0:
  11.2 112.5 all-gather.1
where the time goes:
time: 572 us; the launch traced here: 566 us
  waiting for transfers between devices  258 us (45%)
  local copies, waits for them, and re-layouts  99.6 us (17%)
  matrix products  77.2 us (13%)
  starting transfers between devices  60.2 us (11%)
  other arithmetic  55.6 us (10%)
  between operations  15.4 us (3%)
    all_gather x1, waiting for transfers between devices, per_device(): w_full = lax.all_gather(w_local, 'seq', axis=0, tiled=True)  113 us
    all_to_all x1, waiting for transfers between devices, per_device(): lax.all_to_all(back_sent, 'seq', split_axis=0, concat_axis=0, tiled=True)  48.6 us
    all_to_all x1, waiting for transfers between devices, per_device(): lax.all_to_all(sent, 'seq', split_axis=0, concat_axis=1, tiled=True)[0]  46.1 us
    ppermute x20, waiting for transfers between devices, ring_reduce_scatter(): got = lax.ppermute(buf, 'seq', perm)  35.1 us
    ppermute x20, starting transfers between devices, ring_reduce_scatter(): got = lax.ppermute(buf, 'seq', perm)  27.9 us
    convert_element_type x20, other arithmetic, ring_reduce_scatter(): (got.astype(jnp.float32) + chunk(k + 1).astype(jnp.float32)).astype(jnp.b...  22.7 us
    concatenate x1, local copies, waits for them, and re-layouts, head_pass(): jnp.concatenate([grad_keys, grad_values], axis=-1)  16.1 us
    reshape x1, local copies, waits for them, and re-layouts, head_pass(): jnp.concatenate([grad_keys, grad_values], axis=-1)  16 us
  transfers between devices with their start and end apart: 27, of which 18 were waited for; matrix products, arithmetic and copies ran while one was open for 6% of the time, Pallas kernels for 0%

commit v1 on v0

--- a/solution.py
+++ b/solution.py
@@ -100,7 +100,9 @@
     kv_cols = kv_heads * HD
     all_cols = query_cols + 2 * kv_cols
     w_local = jnp.concatenate([w_query, w_key, w_value], axis=1)
-    w_full = lax.all_gather(w_local, "seq", axis=0, tiled=True)
+    w_full = jnp.concatenate(
+        lax.all_to_all(jnp.stack([w_local] * lax.axis_size("seq")), "seq", 0, 0), axis=0
+    )
     projected = jnp.dot(tokens, w_full, preferred_element_type=jnp.float32).astype(jnp.bfloat16)
     queries = projected[:, :query_cols]
     key_proj = projected[:, query_cols : query_cols + kv_cols]

time: 572 us -> 707 us (1.24)
  waiting for transfers between devices: 258 us -> 383 us
  starting transfers between devices: 60.2 us -> 80 us
  between operations: 15.4 us -> 2.23 us
    all_to_all x0 -> x1, waiting for transfers between devices: none -> 238 us  [per_device(): lax.all_to_all(jnp.stack([w_local] * lax.axis_size('seq')), 'seq', 0, 0)]
    all_gather x1 -> x0, waiting for transfers between devices: 113 us -> none  [per_device(): w_full = lax.all_gather(w_local, 'seq', axis=0, tiled=True)]
    all_to_all x0 -> x1, starting transfers between devices: none -> 12.3 us  [per_device(): lax.all_to_all(jnp.stack([w_local] * lax.axis_size('seq')), 'seq', 0, 0)]
    all_to_all x1, starting transfers between devices: 5.61 us -> 13.3 us  [per_device(): lax.all_to_all(sent, 'seq', split_axis=0, concat_axis=1, tiled=True)[0]]
  transfers between devices with their start and end apart: 27 -> 27, of which waited for: 18 -> 17; matrix products, arithmetic and copies ran while one was open for 6% -> 5% of each run, Pallas kernels for 0% -> 0%
where the time goes in v1:
time: 707 us; the launch traced here: 701 us
  waiting for transfers between devices  383 us (54%)
  local copies, waits for them, and re-layouts  104 us (15%)
  starting transfers between devices  80 us (11%)
  matrix products  77.2 us (11%)
  other arithmetic  54.9 us (8%)
    all_to_all x1, waiting for transfers between devices, per_device(): lax.all_to_all(jnp.stack([w_local] * lax.axis_size('seq')), 'seq', 0, 0)  238 us
    all_to_all x1, waiting for transfers between devices, per_device(): lax.all_to_all(back_sent, 'seq', split_axis=0, concat_axis=0, tiled=True)  48.6 us
    all_to_all x1, waiting for transfers between devices, per_device(): lax.all_to_all(sent, 'seq', split_axis=0, concat_axis=1, tiled=True)[0]  46.3 us
    ppermute x20, waiting for transfers between devices, ring_reduce_scatter(): got = lax.ppermute(buf, 'seq', perm)  35.3 us
    ppermute x20, starting transfers between devices, ring_reduce_scatter(): got = lax.ppermute(buf, 'seq', perm)  27.8 us
    convert_element_type x20, other arithmetic, ring_reduce_scatter(): (got.astype(jnp.float32) + chunk(k + 1).astype(jnp.float32)).astype(jnp.b...  22.7 us
    concatenate x1, local copies, waits for them, and re-layouts, head_pass(): jnp.concatenate([grad_keys, grad_values], axis=-1)  16.1 us
    reshape x1, local copies, waits for them, and re-layouts, head_pass(): jnp.concatenate([grad_keys, grad_values], axis=-1)  16 us
  transfers between devices with their start and end apart: 27, of which 17 were waited for; matrix products, arithmetic and copies ran while one was open for 5% of the time, Pallas kernels for 0%

profile of v1, /device:TPU:1, one launch (start us, length us, event | category | flops | bytes accessed | tf_op | source)
XLA Modules:
  0.0 701.0 jit_solution(7106950711656195648)
XLA Ops:
  6.9 12.3 %all-to-all-start = ((bf16[32,64,2560]{2,1,0:T(8,128)(2,1)}), bf16[32,64,2560]{2,1,0:T(8,128)(2,1)}, u32[]{:S(2)}, u32[]{:S(2)}) async-start(bf16[32,64,2560]{2,1,0:T(8,128)(2,1)} %stack.2), calls=%async_computation | async-start | bytes 20971520 | tf_op jit(solution)/shard_map/all_to_all | solution.py:104
  19.5 237.8 %all-to-all-done = bf16[32,64,2560]{2,1,0:T(8,128)(2,1)} async-done(((bf16[32,64,2560]{2,1,0:T(8,128)(2,1)}), bf16[32,64,2560]{2,1,0:T(8,128)(2,1)}, u32[]{:S(2)}, u32[]{:S(2)}) %all-to-all-start) | async-done | bytes 10485792 | tf_op jit(solution)/shard_map/all_to_all | solution.py:104
  257.3 6.9 fusion.13
  266.1 13.3 %all-to-all-start.1 = ((bf16[32,128,256]{1,2,0:T(8,128)(2,1)}), bf16[32,128,256]{1,2,0:T(8,128)(2,1)}, u32[]{:S(2)}, u32[]{:S(2)}) async-start(bf16[32,128,256]{1,2,0:T(8,128)(2,1)} %pad_maximum_fusion.1), calls=%async_computation.1 | async-start | bytes 4194304 | tf_op jit(solution)/shard_map/all_to_all | solution.py:118
  281.9 46.3 %all-to-all-done.1 = bf16[32,128,256]{1,2,0:T(8,128)(2,1)} async-done(((bf16[32,128,256]{1,2,0:T(8,128)(2,1)}), bf16[32,128,256]{1,2,0:T(8,128)(2,1)}, u32[]{:S(2)}, u32[]{:S(2)}) %all-to-all-start.1) | async-done | bytes 2097184 | tf_op jit(solution)/shard_map/all_to_all | solution.py:118
  340.2 6.2 copy.122
  346.5 7.8 %reshape.158 = bf16[32,896,64]{1,0,2:T(8,128)(2,1)} reshape(bf16[224,128,64]{1,0,2:T(8,128)(2,1)} %copy.122) | data formatting | bytes 7340032 | tf_op jit(solution)/shard_map/reshape | solution.py:24
  357.2 6.2 copy.127
  363.5 7.8 %reshape.160 = bf16[32,896,64]{1,0,2:T(8,128)(2,1)} reshape(bf16[224,128,64]{1,0,2:T(8,128)(2,1)} %copy.127) | data formatting | bytes 7340032 | tf_op jit(solution)/shard_map/reshape | solution.py:25
  371.3 10.8 %fusion.77 = (f32[32,128]{1,0:T(8,128)S(1)}, f32[32,128,896]{2,1,0:T(8,128)}) fusion(pred[896]{0:T(1024)(128)(4,1)S(1)} %broadcast_bitcast_fusion, bf16[32,128,64]{2,1,0:T(8,128)(2,1)S(1)} %bitcast.153, bf16[32,896,64]{1,0,2:T(8,128)(2,1)} %reshape.158), kind=kOutput, calls=%fused_computation.119 | convolution fusion | flops 484443008 | bytes 18891648 | tf_op jit(solution)/shard_map/sub | solution.py:31
  382.1 9.3 %fusion.31 = bf16[32,128,64]{1,2,0:T(8,128)(2,1)S(1)} fusion(bf16[32,896,64]{1,0,2:T(8,128)(2,1)} %reshape.160, f32[32,128,896]{2,1,0:T(8,128)} %get-tuple-element.49, f32[32,128]{1,0:T(8,128)S(1)} %get-tuple-element.48), kind=kOutput, calls=%fused_computation.42 | convolution fusion | flops 477364224 | bytes 18890752 | tf_op jit(solution)/shard_map/gqk,gke->gqe/dot_general | solution.py:34
  391.4 9.8 %fusion.9 = f32[32,896,64]{1,2,0:T(8,128)} fusion(bf16[32,128,64]{2,1,0:T(8,128)(2,1)S(1)} %bitcast.163, f32[32,128,896]{2,1,0:T(8,128)} %get-tuple-element.49, f32[32,128]{1,0:T(8,128)S(1)} %get-tuple-element.48), kind=kOutput, calls=%fused_computation.22 | convolution fusion | flops 477102080 | bytes 22560768 | tf_op jit(solution)/shard_map/gqk,gqe->gke/dot_general | solution.py:48
  401.2 11.0 %multiply_reduce_fusion = (f32[32,128]{1,0:T(8,128)S(1)}, f32[32,128,896]{2,1,0:T(8,128)}) fusion(f32[32,128,896]{2,1,0:T(8,128)} %get-tuple-element.49, f32[32,128]{1,0:T(8,128)S(1)} %get-tuple-element.48, bf16[32,128,64]{2,1,0:T(8,128)(2,1)S(1)} %bitcast.164, bf16[32,896,64]{1,0,2:T(8,128)(2,1)S(1)} %copy-done.7), kind=kOutput, calls=%fused_computation.9 | convolution fusion | flops 480768000 | bytes 33587200 | tf_op jit(solution)/shard_map/gqe,gke->gqk/dot_general | solution.py:37
  412.2 10.9 %multiply_convert_fusion.1 = bf16[32,128,896]{2,1,0:T(8,128)(2,1)S(1)} fusion(f32[32,128,896]{2,1,0:T(8,128)} %get-tuple-element.51, f32[32,128]{1,0:T(8,128)S(1)} %get-tuple-element.50, f32[32,128,896]{2,1,0:T(8,128)} %get-tuple-element.49, f32[32,128]{1,0:T(8,128)S(1)} %get-tuple-element.48), kind=kLoop, calls=%fused_computation.8 | loop fusion | flops 14680064 | bytes 36732928 | tf_op jit(solution)/shard_map/convert_element_type | solution.py:39
  432.3 10.5 %pad_maximum_fusion = f32[32,896,128]{1,2,0:T(8,128)} fusion(f32[32,896,64]{1,2,0:T(8,128)} %fusion.9, f32[32,896,64]{1,2,0:T(8,128)} %broadcast_multiply_fusion), kind=kLoop, calls=%fused_computation.7 | loop fusion | flops 3670016 | bytes 29360128 | tf_op jit(solution)/shard_map/concatenate | solution.py:49
  442.8 16.1 %copy.136 = f32[32,896,128]{2,1,0:T(8,128)} copy(f32[32,896,128]{1,2,0:T(8,128)} %pad_maximum_fusion) | data formatting | bytes 29360128 | tf_op jit(solution)/shard_map/concatenate | solution.py:49
  459.0 16.0 %reshape.162 = f32[224,16384]{1,0:T(8,128)} reshape(f32[32,896,128]{2,1,0:T(8,128)} %copy.136) | data formatting | bytes 29360128 | tf_op jit(solution)/shard_map/reshape | solution.py:49
  476.6 9.1 %fusion.22 = bf16[32,128,128]{2,0,1:T(8,128)(2,1)S(1)} fusion(s32[224]{0:T(256)S(1)} %eq.47, f32[224,16384]{1,0:T(8,128)} %reshape.162), kind=kOutput, calls=%fused_computation.39 | convolution fusion | flops 1409817600 | bytes 15729536 | tf_op jit(solution)/shard_map/dot_general | solution.py:56
  489.4 7.1 %all-to-all-start.2 = ((bf16[32,128,256]{2,1,0:T(8,128)(2,1)}), bf16[32,128,256]{2,1,0:T(8,128)(2,1)S(1)}, u32[]{:S(2)}, u32[]{:S(2)}) async-start(bf16[32,128,256]{2,1,0:T(8,128)(2,1)} %copy.140), calls=%async_computation.2 | async-start | bytes 4194304 | tf_op jit(solution)/shard_map/all_to_all | solution.py:136
  496.5 48.6 %all-to-all-done.2 = bf16[32,128,256]{2,1,0:T(8,128)(2,1)S(1)} async-done(((bf16[32,128,256]{2,1,0:T(8,128)(2,1)}), bf16[32,128,256]{2,1,0:T(8,128)(2,1)S(1)}, u32[]{:S(2)}, u32[]{:S(2)}) %all-to-all-start.2) | async-done | bytes 2097184 | tf_op jit(solution)/shard_map/all_to_all | solution.py:136
  561.7 8.6 %collective-permute-done = bf16[2048,1280]{1,0:T(8,128)(2,1)} collective-permute-done((bf16[2048,1280]{1,0:T(8,128)(2,1)}, bf16[2048,1280]{1,0:T(8,128)(2,1)}, u32[]{:S(2)}, u32[]{:S(2)}) %collective-permute-start) | collective-permute-done | bytes 5242912 | tf_op jit(solution)/shard_map/ppermute | solution.py:162
  581.3 7.0 collective-permute-done.11
  676.2 13.0 %collective-permute-start.23 = (bf16[64,1280]{1,0:T(8,128)(2,1)S(1)}, bf16[64,1280]{1,0:T(8,128)(2,1)S(1)}, u32[]{:S(2)}, u32[]{:S(2)}) collective-permute-start(bf16[64,1280]{1,0:T(8,128)(2,1)S(1)} %add_convert_fusion), channel_id=1, source_target_pairs={{0,32},{32,0},{64,96},{96,64},{128,160},{160,128},{192,224},{224,1... | collective-permute-start | bytes 491528 | tf_op jit(solution)/shard_map/ppermute | solution.py:174
  689.2 8.5 %fusion.21 = bf16[1,128,2048]{2,1,0:T(8,128)(2,1)} fusion(bf16[2048,2560]{1,0:T(8,128)(2,1)} %bitcast.2, bf16[128,256]{0,1:T(8,128)(2,1)S(1)} %bitcast.166, bf16[128,256]{0,1:T(8,128)(2,1)S(1)} %bitcast.168, bf16[128,2048]{0,1:T(8,128)(2,1)} %bitcast.156), kind=kOutput, calls=%fused_computation.36 | convolution fusion | flops 1344405504 | bytes 11665408 | tf_op jit(solution)/shard_map/dot_general | solution.py:149
  (142 shorter events, 157.7 us)
Async XLA Ops:
  6.9 250.3 %all-to-all-start = ((bf16[32,64,2560]{2,1,0:T(8,128)(2,1)}), bf16[32,64,2560]{2,1,0:T(8,128)(2,1)}, u32[]{:S(2)}, u32[]{:S(2)}) async-start(bf16[32,64,2560]{2,1,0:T(8,128)(2,1)} %stack.2), calls=%async_computation | async-start | bytes 20971520 | tf_op jit(solution)/shard_map/all_to_all | solution.py:104
  266.1 62.1 %all-to-all-start.1 = ((bf16[32,128,256]{1,2,0:T(8,128)(2,1)}), bf16[32,128,256]{1,2,0:T(8,128)(2,1)}, u32[]{:S(2)}, u32[]{:S(2)}) async-start(bf16[32,128,256]{1,2,0:T(8,128)(2,1)} %pad_maximum_fusion.1), calls=%async_computation.1 | async-start | bytes 4194304 | tf_op jit(solution)/shard_map/all_to_all | solution.py:118
  489.4 55.8 %all-to-all-start.2 = ((bf16[32,128,256]{2,1,0:T(8,128)(2,1)}), bf16[32,128,256]{2,1,0:T(8,128)(2,1)S(1)}, u32[]{:S(2)}, u32[]{:S(2)}) async-start(bf16[32,128,256]{2,1,0:T(8,128)(2,1)} %copy.140), calls=%async_computation.2 | async-start | bytes 4194304 | tf_op jit(solution)/shard_map/all_to_all | solution.py:136
  559.3 11.0 %collective-permute-start = (bf16[2048,1280]{1,0:T(8,128)(2,1)}, bf16[2048,1280]{1,0:T(8,128)(2,1)}, u32[]{:S(2)}, u32[]{:S(2)}) collective-permute-start(bf16[2048,1280]{1,0:T(8,128)(2,1)} %dynamic-slice_bitcast_fusion), channel_id=1, source_target_pairs={{0,32},{32,0},{64,96},{96,64},{128,160},{160,128},{192,224},{224,1... | collective-permute-start | bytes 15728648 | tf_op jit(solution)/shard_map/ppermute | solution.py:162
  579.1 9.2 %collective-permute-start.11 = (bf16[4,64,640]{2,1,0:T(8,128)(2,1)}, bf16[4,64,640]{2,1,0:T(8,128)(2,1)}, u32[]{:S(2)}, u32[]{:S(2)}) collective-permute-start(bf16[4,64,640]{2,1,0:T(8,128)(2,1)} %dynamic-slice_bitcast_fusion.1), channel_id=1, source_target_pairs={{1,0},{2,1},{3,2},{4,3},{5,4},{6,5},{7,6},{0,7},{9,8},{10,9},{11,1... | collective-permute-start | bytes 983048 | tf_op jit(solution)/shard_map/ppermute | solution.py:83
  580.5 11.7 %collective-permute-start.1 = (bf16[4,64,640]{2,1,0:T(8,128)(2,1)}, bf16[4,64,640]{2,1,0:T(8,128)(2,1)}, u32[]{:S(2)}, u32[]{:S(2)}) collective-permute-start(bf16[4,64,640]{2,1,0:T(8,128)(2,1)} %dynamic-slice_bitcast_fusion.2), channel_id=1, source_target_pairs={{0,1},{1,2},{2,3},{3,4},{4,5},{5,6},{6,7},{7,0},{8,9},{9,10},{10,1... | collective-permute-start | bytes 983048 | tf_op jit(solution)/shard_map/ppermute | solution.py:83
  590.2 8.7 %collective-permute-start.12 = (bf16[4,64,640]{2,1,0:T(8,128)(2,1)}, bf16[4,64,640]{2,1,0:T(8,128)(2,1)}, u32[]{:S(2)}, u32[]{:S(2)}) collective-permute-start(bf16[4,64,640]{2,1,0:T(8,128)(2,1)} %fusion.46), channel_id=1, source_target_pairs={{1,0},{2,1},{3,2},{4,3},{5,4},{6,5},{7,6},{0,7},{9,8},{10,9},{11,1... | collective-permute-start | bytes 983048 | tf_op jit(solution)/shard_map/ppermute | solution.py:83
  594.0 9.6 %collective-permute-start.2 = (bf16[4,64,640]{2,1,0:T(8,128)(2,1)}, bf16[4,64,640]{2,1,0:T(8,128)(2,1)}, u32[]{:S(2)}, u32[]{:S(2)}) collective-permute-start(bf16[4,64,640]{2,1,0:T(8,128)(2,1)} %fusion.53), channel_id=1, source_target_pairs={{0,1},{1,2},{2,3},{3,4},{4,5},{5,6},{6,7},{7,0},{8,9},{9,10},{10,1... | collective-permute-start | bytes 983048 | tf_op jit(solution)/shard_map/ppermute | solution.py:83
  600.7 8.1 %collective-permute-start.13 = (bf16[4,64,640]{2,1,0:T(8,128)(2,1)}, bf16[4,64,640]{2,1,0:T(8,128)(2,1)}, u32[]{:S(2)}, u32[]{:S(2)}) collective-permute-start(bf16[4,64,640]{2,1,0:T(8,128)(2,1)} %fusion.45), channel_id=1, source_target_pairs={{1,0},{2,1},{3,2},{4,3},{5,4},{6,5},{7,6},{0,7},{9,8},{10,9},{11,1... | collective-permute-start | bytes 983048 | tf_op jit(solution)/shard_map/ppermute | solution.py:83
  605.4 8.7 %collective-permute-start.3 = (bf16[4,64,640]{2,1,0:T(8,128)(2,1)}, bf16[4,64,640]{2,1,0:T(8,128)(2,1)}, u32[]{:S(2)}, u32[]{:S(2)}) collective-permute-start(bf16[4,64,640]{2,1,0:T(8,128)(2,1)} %fusion.52), channel_id=1, source_target_pairs={{0,1},{1,2},{2,3},{3,4},{4,5},{5,6},{6,7},{7,0},{8,9},{9,10},{10,1... | collective-permute-start | bytes 983048 | tf_op jit(solution)/shard_map/ppermute | solution.py:83
  610.7 7.7 %collective-permute-start.14 = (bf16[4,64,640]{2,1,0:T(8,128)(2,1)}, bf16[4,64,640]{2,1,0:T(8,128)(2,1)}, u32[]{:S(2)}, u32[]{:S(2)}) collective-permute-start(bf16[4,64,640]{2,1,0:T(8,128)(2,1)} %fusion.44), channel_id=1, source_target_pairs={{1,0},{2,1},{3,2},{4,3},{5,4},{6,5},{7,6},{0,7},{9,8},{10,9},{11,1... | collective-permute-start | bytes 983048 | tf_op jit(solution)/shard_map/ppermute | solution.py:83
  615.9 7.5 %collective-permute-start.4 = (bf16[4,64,640]{2,1,0:T(8,128)(2,1)}, bf16[4,64,640]{2,1,0:T(8,128)(2,1)}, u32[]{:S(2)}, u32[]{:S(2)}) collective-permute-start(bf16[4,64,640]{2,1,0:T(8,128)(2,1)} %fusion.51), channel_id=1, source_target_pairs={{0,1},{1,2},{2,3},{3,4},{4,5},{5,6},{6,7},{7,0},{8,9},{9,10},{10,1... | collective-permute-start | bytes 983048 | tf_op jit(solution)/shard_map/ppermute | solution.py:83
  620.3 7.5 %collective-permute-start.15 = (bf16[4,64,640]{2,1,0:T(8,128)(2,1)}, bf16[4,64,640]{2,1,0:T(8,128)(2,1)}, u32[]{:S(2)}, u32[]{:S(2)}) collective-permute-start(bf16[4,64,640]{2,1,0:T(8,128)(2,1)} %fusion.43), channel_id=1, source_target_pairs={{1,0},{2,1},{3,2},{4,3},{5,4},{6,5},{7,6},{0,7},{9,8},{10,9},{11,1... | collective-permute-start | bytes 983048 | tf_op jit(solution)/shard_map/ppermute | solution.py:83
  625.3 7.5 %collective-permute-start.5 = (bf16[4,64,640]{2,1,0:T(8,128)(2,1)}, bf16[4,64,640]{2,1,0:T(8,128)(2,1)}, u32[]{:S(2)}, u32[]{:S(2)}) collective-permute-start(bf16[4,64,640]{2,1,0:T(8,128)(2,1)} %fusion.50), channel_id=1, source_target_pairs={{0,1},{1,2},{2,3},{3,4},{4,5},{5,6},{6,7},{7,0},{8,9},{9,10},{10,1... | collective-permute-start | bytes 983048 | tf_op jit(solution)/shard_map/ppermute | solution.py:83
  629.7 7.5 %collective-permute-start.16 = (bf16[4,64,640]{2,1,0:T(8,128)(2,1)}, bf16[4,64,640]{2,1,0:T(8,128)(2,1)}, u32[]{:S(2)}, u32[]{:S(2)}) collective-permute-start(bf16[4,64,640]{2,1,0:T(8,128)(2,1)} %fusion.42), channel_id=1, source_target_pairs={{1,0},{2,1},{3,2},{4,3},{5,4},{6,5},{7,6},{0,7},{9,8},{10,9},{11,1... | collective-permute-start | bytes 983048 | tf_op jit(solution)/shard_map/ppermute | solution.py:83
  634.6 7.5 %collective-permute-start.6 = (bf16[4,64,640]{2,1,0:T(8,128)(2,1)}, bf16[4,64,640]{2,1,0:T(8,128)(2,1)}, u32[]{:S(2)}, u32[]{:S(2)}) collective-permute-start(bf16[4,64,640]{2,1,0:T(8,128)(2,1)} %fusion.49), channel_id=1, source_target_pairs={{0,1},{1,2},{2,3},{3,4},{4,5},{5,6},{6,7},{7,0},{8,9},{9,10},{10,1... | collective-permute-start | bytes 983048 | tf_op jit(solution)/shard_map/ppermute | solution.py:83
  639.0 7.5 %collective-permute-start.17 = (bf16[4,64,640]{2,1,0:T(8,128)(2,1)}, bf16[4,64,640]{2,1,0:T(8,128)(2,1)}, u32[]{:S(2)}, u32[]{:S(2)}) collective-permute-start(bf16[4,64,640]{2,1,0:T(8,128)(2,1)} %fusion.41), channel_id=1, source_target_pairs={{1,0},{2,1},{3,2},{4,3},{5,4},{6,5},{7,6},{0,7},{9,8},{10,9},{11,1... | collective-permute-start | bytes 983048 | tf_op jit(solution)/shard_map/ppermute | solution.py:83
  643.2 8.4 %collective-permute-start.7 = (bf16[4,64,640]{2,1,0:T(8,128)(2,1)S(1)}, bf16[4,64,640]{2,1,0:T(8,128)(2,1)S(1)}, u32[]{:S(2)}, u32[]{:S(2)}) collective-permute-start(bf16[4,64,640]{2,1,0:T(8,128)(2,1)S(1)} %fusion.48), channel_id=1, source_target_pairs={{0,1},{1,2},{2,3},{3,4},{4,5},{5,6},{6,7},{7,0},{8,9},{9,10},{10,1... | collective-permute-start | bytes 983048 | tf_op jit(solution)/shard_map/ppermute | solution.py:83
  647.6 5.1 collective-permute-start.18
  651.7 4.9 collective-permute-start.8
  656.6 4.6 collective-permute-start.9
  661.2 4.6 collective-permute-start.10
  670.4 5.8 collective-permute-start.22
  676.2 22.9 %collective-permute-start.23 = (bf16[64,1280]{1,0:T(8,128)(2,1)S(1)}, bf16[64,1280]{1,0:T(8,128)(2,1)S(1)}, u32[]{:S(2)}, u32[]{:S(2)}) collective-permute-start(bf16[64,1280]{1,0:T(8,128)(2,1)S(1)} %add_convert_fusion), channel_id=1, source_target_pairs={{0,32},{32,0},{64,96},{96,64},{128,160},{160,128},{192,224},{224,1... | collective-permute-start | bytes 491528 | tf_op jit(solution)/shard_map/ppermute | solution.py:174
  (15 other events, 384.7 us)
